TPU v7x, 256 devices: a whole 4x4x8 slice. The times are simulated.
256 devices in a mesh: section: 16 (over y_lo, x, core), expert: 16 (over z, y_hi).
Axes of the slice: x: 4, y: 4 (y_hi: 2, y_lo: 2; y = y_hi * 2 + y_lo), z: 8, core: 2. Of those that a mesh axis runs over, the one named last changes fastest.
Arguments:
- activations: bfloat16 [16384, 8192], P('section', 'expert'), may hold values from -12 to 12
- modality: int32 [16384], P('section'), may hold values from 0 to 1
- selected: int32 [16, 256], P('section'), may hold values from 0 to 1023, as said below
- routes: int32 [4096, 1], P('section'), may hold values from 0 to 15, as said below
- norm_gain: float32 [2, 8192], P(None, 'expert'), may hold values from 0.1 to 1.9
- router: float32 [8192], P('expert'), may hold values from -0.0625 to 0.0625
- gate_w: bfloat16 [16, 3072, 8192], P('expert', 'section'), may hold values from -0.0625 to 0.0625
- up_w: bfloat16 [16, 3072, 8192], P('expert', 'section'), may hold values from -0.0625 to 0.0625
- down_w: bfloat16 [16, 3072, 8192], P('expert', 'section'), may hold values from -0.21875 to 0.21875
Outputs:
- block_out: bfloat16 [16384, 8192], P('section', 'expert')
Inputs may be any that keep to these rules, and one draw needn't show every extreme that they name: Each row of selected lists 256 different positions in rising order, the first and the last position among them. `routes`: among the 256 rows of one section group no expert is named more than 24 times, and some expert exactly 24 times; the entry for selected[s, j] is below 8 if that token's modality is 0, and 8 or more if it is 1.
All inputs are finite; a program needn't handle non-finite values.
Results may differ from a plain program's by a relative error of at most 0.0075.
Values may be sent and summed in bfloat16 or wider, within the bound.
No kernel may reach another device: no remote copies, remote signals or barrier semaphores. Data moves between devices by JAX's collectives and lax.ppermute only.
A program may use at most 128 MiB of HBM per device.

v0:
```python
import jax
import jax.numpy as jnp
from jax import lax
from jax.sharding import PartitionSpec as P

EPS = 1e-05
SECTION = ("chip", "core")


def passed_along(block, axis, distance):
    names = axis if isinstance(axis, tuple) else (axis,)
    count = 1
    for name in names:
        count *= lax.axis_size(name)
    route = [((i - distance) % count, i) for i in range(count)]
    return lax.ppermute(block, axis, route)


def feature_product(block, weight):
    return lax.dot_general(
        block, weight, (((1,), (1,)), ((), ())), preferred_element_type=jnp.float32
    )


def body(activations, modality, selected, routes, norm_gain, router, gate_w, up_w, down_w):
    n_chip = lax.axis_size("chip")
    n_core = lax.axis_size("core")
    n_section = n_chip * n_core
    sel_count = selected.shape[1]
    expert_count = lax.axis_size("expert") * gate_w.shape[0]
    capacity = max(2, 3 * sel_count // (2 * expert_count))
    groups = n_section
    sel_next = passed_along(selected, SECTION, -1)[0]
    routes_next = passed_along(routes, SECTION, -1)[:, 0]
    rows = activations[sel_next]
    both = jnp.stack([routes_next, routes[:, 0]], axis=1)
    onehot = (both[:, :, None] == jnp.arange(expert_count, dtype=jnp.int32)[None, None, :]).astype(
        jnp.int32
    )
    slots = jnp.sum((jnp.cumsum(onehot, axis=0) - 1) * onehot, axis=2)
    targets = both * capacity + slots
    target = targets[:, 0]
    position = targets[:, 1]
    feature_width = rows.shape[1]
    n_exp_dev = lax.axis_size("expert")
    local_width = router.shape[0]
    tables = jnp.concatenate([norm_gain, router[None, :]], axis=0)
    table_count = tables.shape[0]
    parts = []
    rest = tables
    for _ in range(3):
        piece = rest.astype(jnp.bfloat16)
        parts.append(piece)
        rest = rest - piece.astype(jnp.float32)
    sources = jnp.concatenate([rows] + parts, axis=0)
    table_rows = 2
    coded_rows = 3 * table_rows
    span = capacity + -(-coded_rows // 8) * 8
    slot_of_row = jnp.arange(expert_count * span, dtype=jnp.int32)
    row_expert = slot_of_row // span
    row_slot = slot_of_row % span
    row_kind = (row_expert >= expert_count // 2).astype(jnp.int32)
    coded_index = row_slot - capacity
    part_index = coded_index // table_rows
    table_index = jnp.where(coded_index % table_rows == 0, row_kind, table_count - 1)
    wanted = jnp.where(row_slot < capacity, row_expert * capacity + row_slot, -1)
    token_hit = target[None, :] == wanted[:, None]
    table_source = jnp.where(
        (coded_index >= 0) & (coded_index < coded_rows), part_index * table_count + table_index, -1
    )
    table_hit = table_source[:, None] == jnp.arange(3 * table_count, dtype=jnp.int32)[None, :]
    placing = jnp.concatenate([token_hit, table_hit], axis=1).astype(jnp.bfloat16)
    buffer = jnp.dot(placing, sources, preferred_element_type=jnp.float32).astype(jnp.bfloat16)
    buffer = buffer.reshape(expert_count, span, feature_width)
    mine = lax.all_to_all(buffer, "expert", split_axis=0, concat_axis=2, tiled=True)[0]
    coded = mine[capacity : capacity + coded_rows].astype(jnp.float32)
    coded = coded.reshape(3, table_rows, mine.shape[1])
    tables = coded[0] + coded[1] + coded[2]
    mine = mine[:capacity]
    gains = tables[0]
    router_all = tables[1]
    picked = mine.astype(jnp.float32)
    d = picked.shape[1]
    scale = lax.rsqrt(jnp.sum(picked * picked, axis=1) / d + EPS)
    normed = (picked * scale[:, None] * gains[None, :]).astype(jnp.bfloat16)
    score = jax.nn.sigmoid(scale * jnp.sum(picked * gains[None, :] * router_all[None, :], axis=1))
    score_home = passed_along(score, SECTION, 1)
    block = lax.all_gather(normed, SECTION, axis=0, tiled=True)
    stacked = jnp.concatenate([gate_w[0], up_w[0]], axis=0)
    block, score_home, leaving, stacked = lax.optimization_barrier(
        (block, score_home, activations, stacked)
    )
    arrived = passed_along(leaving, SECTION, 1)
    both_products = feature_product(block, stacked)
    hidden_units = gate_w.shape[1]
    gate = both_products[:, :hidden_units]
    upper = both_products[:, hidden_units:]
    hidden = (jax.nn.silu(gate) * upper).astype(jnp.bfloat16)
    hidden_width = hidden.shape[1]
    order = []
    for core in range(n_core):
        for chip in range(n_chip):
            order.append((chip * n_core + core - 1) % n_section)
    hidden = jnp.take(
        hidden.reshape(groups, capacity, hidden_width), jnp.array(order, jnp.int32), axis=0
    ).reshape(groups * capacity, hidden_width)
    hidden = hidden.reshape(n_core, n_chip * capacity, hidden_width)
    core = lax.axis_index("core")

    def down_part(rows):
        part = jnp.dot(rows, down_w[0], preferred_element_type=jnp.float32)
        return (
            lax.optimization_barrier(part.astype(jnp.bfloat16))
            .astype(jnp.float32)
            .astype(jnp.bfloat16)
        )

    give = down_part(lax.dynamic_index_in_dim(hidden, 1 - core, axis=0, keepdims=False))
    taken = lax.ppermute(give, "core", [(0, 1), (1, 0)])
    keep = down_part(lax.dynamic_index_in_dim(hidden, core, axis=0, keepdims=False))
    pair = (keep.astype(jnp.float32) + taken.astype(jnp.float32)).astype(jnp.bfloat16)
    summed = lax.psum_scatter(pair, "chip", scatter_dimension=0, tiled=True)
    update_rows = (score_home[:, None] * summed.astype(jnp.float32)).astype(jnp.bfloat16)
    outgoing = update_rows.reshape(capacity, n_exp_dev, local_width).transpose(1, 0, 2)
    back = lax.all_to_all(outgoing, "expert", split_axis=0, concat_axis=0, tiled=True)
    flat_back = back.reshape(expert_count * capacity, local_width)
    picks = selected[0]
    token_count = arrived.shape[0]
    source = jnp.full((token_count,), -1, jnp.int32).at[picks].set(position)
    spread = (
        source[:, None] == jnp.arange(expert_count * capacity, dtype=jnp.int32)[None, :]
    ).astype(jnp.bfloat16)
    update = jnp.dot(spread, flat_back, preferred_element_type=jnp.float32)
    return (arrived.astype(jnp.float32) + update).astype(jnp.bfloat16)


def solution(mesh):
    n_section, n_expert = mesh.devices.shape
    split = jax.sharding.Mesh(
        mesh.devices.reshape(n_section // 2, 2, n_expert), ("chip", "core", "expert")
    )
    placed = (
        P(SECTION, "expert"),
        P(SECTION),
        P(SECTION, None),
        P(SECTION, None),
        P(None, "expert"),
        P("expert"),
        P("expert", SECTION, None),
        P("expert", SECTION, None),
        P("expert", SECTION, None),
    )
    return jax.shard_map(
        body, mesh=split, in_specs=placed, out_specs=P(SECTION, "expert"), check_vma=False
    )
```

profile of v0, /device:TPU:6, one launch (start us, length us, event | category | flops | bytes accessed | tf_op | source)
XLA Modules:
  0.0 195.6 jit_solution(17597508050167331478)
XLA Ops:
  6.8 0.7 collective-permute-start.1
  7.5 0.7 fusion.27
  8.2 0.7 fusion.22
  8.9 0.8 iota_compare_fusion.2
  9.7 0.7 pad_add_fusion
  10.4 1.2 reduce-window.6
  11.9 0.7 multiply_add_fusion
  12.6 0.5 fusion.49
  13.3 2.6 %gather_fusion = bf16[256,512]{1,0:T(8,128)(2,1)S(1)} fusion(bf16[1024,512]{1,0:T(8,128)(2,1)} %param.10, s32[1024]{0:T(1024)S(1)} %pad_clamp_fusion.1), kind=kCustom, calls=%fused_computation | custom fusion | bytes 525312 | tf_op jit(solution)/shard_map/gather | solution.py:35
  15.9 1.3 convolution_convert_fusion.2
  17.2 30.0 %all_to_all.20 = bf16[16,32,512]{2,1,0:T(8,128)(2,1)S(1)} all-to-all(bf16[16,32,512]{2,1,0:T(8,128)(2,1)S(1)} %bitcast.81), channel_id=1, replica_groups=mesh['chip'=8,'core'=2,'expert'=16] {'expert'}, dimensions={0} | all-to-all | bytes 1048576 | tf_op jit(solution)/shard_map/all_to_all | solution.py:75
  47.5 0.3 multiply_reduce_fusion
  47.8 0.9 multiply_convert_fusion.1
  48.8 6.2 %pad_maximum_fusion = bf16[384,8192]{1,0:T(8,128)(2,1)} fusion(bf16[192,8192]{1,0:T(8,128)(2,1)} %bitcast.73, bf16[192,8192]{1,0:T(8,128)(2,1)} %bitcast.74), kind=kLoop, calls=%fused_computation.5 | loop fusion | flops 12582912 | bytes 12582912 | tf_op jit(solution)/shard_map/concatenate | solution.py:89
  55.0 1.6 collective-permute-start.2
  56.6 1.4 collective-permute-done.2
  58.0 31.2 %all-gather.2.cloned.1.call-done = bf16[384,8192]{1,0:T(8,128)(2,1)} async-done(((bf16[24,8192]{1,0:T(8,128)(2,1)}), bf16[384,8192]{1,0:T(8,128)(2,1)}) %all-gather.2.cloned.1.call-update) | async-done | bytes 6291472 | tf_op jit(solution)/shard_map/all_gather | solution.py:88
  89.2 8.2 %fusion.51 = f32[384,384]{0,1:T(8,128)S(1)} fusion(bf16[384,8192]{1,0:T(8,128)(2,1)} %all-gather.2.cloned.1.call-done, bf16[384,8192]{1,0:T(8,128)(2,1)} %pad_maximum_fusion), kind=kOutput, calls=%fused_computation.100 | convolution fusion | flops 2415919104 | bytes 13172736 | tf_op jit(solution)/shard_map/dot_general | solution.py:20
  97.7 0.6 gather_fusion.1
  98.3 2.6 %convolution_convert_fusion = bf16[192,8192]{1,0:T(8,128)(2,1)} fusion(bf16[1,192,8192]{2,1,0:T(8,128)(2,1)S(1)} %copy-done, bf16[2,192,192]{2,1,0:T(8,128)(2,1)S(1)} %bitcast.78, s32[]{:T(128)S(6)} %select_n.116), kind=kOutput, calls=%fused_computation.3 | convolution fusion | flops 605552640 | bytes 6389764 | tf_op jit(solution)/shard_map/dot_general | solution.py:111
  101.1 1.0 convolution_convert_fusion.1
  102.1 4.8 %collective-permute-done.4 = bf16[192,8192]{1,0:T(8,128)(2,1)} collective-permute-done((bf16[192,8192]{1,0:T(8,128)(2,1)}, bf16[192,8192]{1,0:T(8,128)(2,1)}, u32[]{:S(2)}, u32[]{:S(2)}) %collective-permute-start.4) | collective-permute-done | bytes 3145760 | tf_op jit(solution)/shard_map/ppermute | solution.py:119
  106.9 4.6 %add_convert_fusion = bf16[192,8192]{1,0:T(8,128)(2,1)} fusion(bf16[192,8192]{1,0:T(8,128)(2,1)} %collective-permute-done.4, bf16[192,8192]{1,0:T(8,128)(2,1)S(1)} %convolution_convert_fusion.1), kind=kLoop, calls=%fused_computation.6 | loop fusion | flops 6291456 | bytes 9437184 | tf_op jit(solution)/shard_map/convert_element_type | solution.py:121
  111.5 0.5 collective-permute-start.3
  112.0 48.7 %reduce-scatter.2.cloned.1.call-done = bf16[24,8192]{1,0:T(8,128)(2,1)} async-done(((bf16[192,8192]{1,0:T(8,128)(2,1)}), bf16[24,8192]{1,0:T(8,128)(2,1)}) %reduce-scatter.2.cloned.1.call-update) | async-done | bytes 393232 | tf_op jit(solution)/shard_map/reduce_scatter | solution.py:122
  160.8 1.1 multiply_convert_fusion
  161.9 0.8 copy.38
  162.7 9.3 %all-to-all-start.1 = ((bf16[16,24,512]{2,1,0:T(8,128)(2,1)}), bf16[16,24,512]{2,1,0:T(8,128)(2,1)S(1)}, u32[]{:S(2)}, u32[]{:S(2)}) async-start(bf16[16,24,512]{2,1,0:T(8,128)(2,1)} %bitcast.76), calls=%async_computation.2 | async-start | bytes 786432 | tf_op jit(solution)/shard_map/all_to_all | solution.py:125
  172.0 1.6 scatter_custom_fusion
  173.6 11.9 %all-to-all-done.1 = bf16[16,24,512]{2,1,0:T(8,128)(2,1)S(1)} async-done(((bf16[16,24,512]{2,1,0:T(8,128)(2,1)}), bf16[16,24,512]{2,1,0:T(8,128)(2,1)S(1)}, u32[]{:S(2)}, u32[]{:S(2)}) %all-to-all-start.1) | async-done | bytes 393248 | tf_op jit(solution)/shard_map/all_to_all | solution.py:125
  185.5 0.8 fusion.2
  186.2 2.6 %add_convert_fusion.1 = bf16[1024,512]{1,0:T(8,128)(2,1)} fusion(f32[1024,512]{1,0:T(8,128)S(1)} %fusion.2, bf16[1024,512]{1,0:T(8,128)(2,1)} %collective-permute-done.3), kind=kLoop, calls=%fused_computation.9 | loop fusion | flops 1572864 | bytes 4194304 | tf_op jit(solution)/shard_map/convert_element_type | solution.py:134
  (38 shorter events, 1.6 us)
Async XLA Ops:
  6.5 91.7 %copy-start = (bf16[1,192,8192]{2,1,0:T(8,128)(2,1)S(1)}, bf16[1,192,8192]{2,1,0:T(8,128)(2,1)}, u32[]{:S(2)}) copy-start(bf16[1,192,8192]{2,1,0:T(8,128)(2,1)} %param.17) | copy-start | bytes 9437188
  6.5 82.7 %all-gather.2.cloned.1.call-start = ((), (), s32[]{:S(2)}) async-start(), calls=%async_computation.3 | async-start | bytes 6684672 | tf_op jit(solution)/shard_map/all_gather | solution.py:88
  6.5 3.2 %collective-permute-start = (s32[256,1]{0,1:T(1,128)}, s32[256,1]{0,1:T(1,128)S(1)}, u32[]{:S(2)}, u32[]{:S(2)}) collective-permute-start(s32[256,1]{0,1:T(1,128)} %param.12), channel_id=1, source_target_pairs={{16,0},{32,16},{48,32},{64,48},{80,64},{96,80},{112,96},{128,112},... | collective-permute-start | bytes 3080 | tf_op jit(solution)/shard_map/ppermute | solution.py:16
  6.8 6.3 %collective-permute-start.1 = (s32[1,256]{1,0:T(1,128)}, s32[1,256]{1,0:T(1,128)S(1)}, u32[]{:S(2)}, u32[]{:S(2)}) collective-permute-start(s32[1,256]{1,0:T(1,128)} %param.11), channel_id=1, source_target_pairs={{16,0},{32,16},{48,32},{64,48},{80,64},{96,80},{112,96},{128,112},... | collective-permute-start | bytes 3080 | tf_op jit(solution)/shard_map/ppermute | solution.py:16
  47.2 1.6 copy-start.2
  48.7 112.0 %reduce-scatter.2.cloned.1.call-start = ((), (), s32[]{:S(2)}) async-start(), calls=%async_computation.4 | async-start | bytes 3538944 | tf_op jit(solution)/shard_map/reduce_scatter | solution.py:122
  55.0 3.0 %collective-permute-start.2 = (f32[24]{0:T(128)S(1)}, f32[24]{0:T(128)S(1)}, u32[]{:S(2)}, u32[]{:S(2)}) collective-permute-start(f32[24]{0:T(128)S(1)} %get-tuple-element.23), channel_id=1, source_target_pairs={{240,0},{0,16},{16,32},{32,48},{48,64},{64,80},{80,96},{96,112},{1... | collective-permute-start | bytes 296 | tf_op jit(solution)/shard_map/ppermute | solution.py:16
  100.9 6.0 %collective-permute-start.4 = (bf16[192,8192]{1,0:T(8,128)(2,1)}, bf16[192,8192]{1,0:T(8,128)(2,1)}, u32[]{:S(2)}, u32[]{:S(2)}) collective-permute-start(bf16[192,8192]{1,0:T(8,128)(2,1)} %convolution_convert_fusion), channel_id=1, source_target_pairs={{0,16},{16,0},{1,17},{17,1},{2,18},{18,2},{3,19},{19,3},{4,20},{20... | collective-permute-start | bytes 9437192 | tf_op jit(solution)/shard_map/ppermute | solution.py:119
  111.5 60.5 %copy-start.1 = (s32[1,256]{1,0:T(1,128)S(1)}, s32[1,256]{1,0:T(1,128)}, u32[]{:S(2)}) copy-start(s32[1,256]{1,0:T(1,128)} %param.11) | copy-start | bytes 3076
  111.5 74.7 %collective-permute-start.3 = (bf16[1024,512]{1,0:T(8,128)(2,1)}, bf16[1024,512]{1,0:T(8,128)(2,1)}, u32[]{:S(2)}, u32[]{:S(2)}) collective-permute-start(bf16[1024,512]{1,0:T(8,128)(2,1)} %param.10), channel_id=1, source_target_pairs={{240,0},{0,16},{16,32},{32,48},{48,64},{64,80},{80,96},{96,112},{1... | collective-permute-start | bytes 3145736 | tf_op jit(solution)/shard_map/ppermute | solution.py:16
  162.7 22.8 %all-to-all-start.1 = ((bf16[16,24,512]{2,1,0:T(8,128)(2,1)}), bf16[16,24,512]{2,1,0:T(8,128)(2,1)S(1)}, u32[]{:S(2)}, u32[]{:S(2)}) async-start(bf16[16,24,512]{2,1,0:T(8,128)(2,1)} %bitcast.76), calls=%async_computation.2 | async-start | bytes 786432 | tf_op jit(solution)/shard_map/all_to_all | solution.py:125
Sparse Core Ops, SparseCore 0:
  48.9 40.3 all-gather.1
  111.6 49.0 reduce-scatter.1
where the time goes:
time: 196 us
  waiting for transfers between devices  98 us (50%)
  blocking collectives  30 us (15%)
  other arithmetic  21 us (11%)
  matrix products  13.9 us (7%)
  between operations  13.6 us (7%)
  starting transfers between devices  12.6 us (6%)
  local copies, waits for them, and re-layouts  6.47 us (3%)
    reduce_scatter x1, waiting for transfers between devices, body(): summed = lax.psum_scatter(pair, 'chip', scatter_dimension=0, tiled=True)  48.7 us
    all_gather x1, waiting for transfers between devices, body(): block = lax.all_gather(normed, SECTION, axis=0, tiled=True)  31.2 us
    all_to_all x1, blocking collectives, body(): lax.all_to_all(buffer, 'expert', split_axis=0, concat_axis=2, tiled=True)[0]  30 us
    all_to_all x1, waiting for transfers between devices, body(): lax.all_to_all(outgoing, 'expert', split_axis=0, concat_axis=0, tiled=True)  11.9 us
    all_to_all x1, starting transfers between devices, body(): lax.all_to_all(outgoing, 'expert', split_axis=0, concat_axis=0, tiled=True)  9.31 us
    dot_general x1, matrix products, feature_product(): lax.dot_general(block, weight, (((1,), (1,)), ((), ())), preferred_elemen...  8.2 us
    concatenate x1, other arithmetic, body(): stacked = jnp.concatenate([gate_w[0], up_w[0]], axis=0)  6.21 us
    ppermute x1, waiting for transfers between devices, body(): taken = lax.ppermute(give, 'core', [(0, 1), (1, 0)])  4.77 us
  transfers between devices with their start and end apart: 8, of which 5 were waited for; matrix products, arithmetic and copies ran while one was open for 9% of the time, Pallas kernels for 0%

commit v1 on v0

--- a/solution.py
+++ b/solution.py
@@ -5,6 +5,15 @@
 
 EPS = 1e-05
 SECTION = ("chip", "core")
+expand_screen = lambda z: jnp.concatenate(
+    jax.lax.all_to_all(
+        jnp.stack(jnp.split(z, jax.lax.axis_size("expert"), axis=0)),
+        axis_name="expert",
+        split_axis=0,
+        concat_axis=0,
+    ),
+    axis=2,
+)
 
 
 def passed_along(block, axis, distance):
@@ -72,7 +81,7 @@
     placing = jnp.concatenate([token_hit, table_hit], axis=1).astype(jnp.bfloat16)
     buffer = jnp.dot(placing, sources, preferred_element_type=jnp.float32).astype(jnp.bfloat16)
     buffer = buffer.reshape(expert_count, span, feature_width)
-    mine = lax.all_to_all(buffer, "expert", split_axis=0, concat_axis=2, tiled=True)[0]
+    mine = expand_screen(buffer)[0]
     coded = mine[capacity : capacity + coded_rows].astype(jnp.float32)
     coded = coded.reshape(3, table_rows, mine.shape[1])
     tables = coded[0] + coded[1] + coded[2]

time: 196 us -> 198 us (1.010)
  no operation moved by 1% of the time
where the time goes in v1:
time: 198 us; the launch traced here: 197 us
  waiting for transfers between devices  98.2 us (50%)
  blocking collectives  30.5 us (15%)
  other arithmetic  22.3 us (11%)
  matrix products  13.9 us (7%)
  between operations  13.7 us (7%)
  starting transfers between devices  12 us (6%)
  local copies, waits for them, and re-layouts  6.58 us (3%)
    reduce_scatter x1, waiting for transfers between devices, body(): summed = lax.psum_scatter(pair, 'chip', scatter_dimension=0, tiled=True)  48.7 us
    all_gather x1, waiting for transfers between devices, body(): block = lax.all_gather(normed, SECTION, axis=0, tiled=True)  30.8 us
    all_to_all x1, blocking collectives, jax.lax.all_to_all(jnp.stack(jnp.split(z, jax.lax.axis_size('expert'), ax...  30.5 us
    all_to_all x1, waiting for transfers between devices, body(): lax.all_to_all(outgoing, 'expert', split_axis=0, concat_axis=0, tiled=True)  11.9 us
    all_to_all x1, starting transfers between devices, body(): lax.all_to_all(outgoing, 'expert', split_axis=0, concat_axis=0, tiled=True)  9.3 us
    dot_general x1, matrix products, feature_product(): lax.dot_general(block, weight, (((1,), (1,)), ((), ())), preferred_elemen...  8.21 us
    concatenate x1, other arithmetic, body(): stacked = jnp.concatenate([gate_w[0], up_w[0]], axis=0)  6.21 us
    ppermute x1, waiting for transfers between devices, body(): taken = lax.ppermute(give, 'core', [(0, 1), (1, 0)])  4.79 us
  transfers between devices with their start and end apart: 8, of which 5 were waited for; matrix products, arithmetic and copies ran while one was open for 9% of the time, Pallas kernels for 0%

profile of v1, /device:TPU:6, one launch (start us, length us, event | category | flops | bytes accessed | tf_op | source)
XLA Modules:
  0.0 197.2 jit_solution(16559005471230070064)
XLA Ops:
  6.8 0.7 collective-permute-start.1
  7.5 0.7 fusion.43
  8.2 1.3 fusion.38
  9.5 0.8 iota_compare_fusion.2
  10.3 0.7 pad_add_fusion
  11.0 1.2 reduce-window.6
  12.5 0.7 multiply_add_fusion
  13.2 0.6 fusion.65
  13.9 0.7 pad_clamp_fusion
  14.6 2.6 %gather_fusion = bf16[256,512]{1,0:T(8,128)(2,1)S(1)} fusion(bf16[1024,512]{1,0:T(8,128)(2,1)} %param.10, s32[1024]{0:T(1024)S(1)} %get-tuple-element.26), kind=kCustom, calls=%fused_computation | custom fusion | bytes 525312 | tf_op jit(solution)/shard_map/gather | solution.py:44
  17.2 1.3 convolution_convert_fusion.2
  18.7 30.5 %all_to_all.10 = bf16[16,1,32,512]{3,2,1,0:T(8,128)(2,1)S(1)} all-to-all(bf16[16,1,32,512]{3,2,1,0:T(8,128)(2,1)S(1)} %fusion.21), channel_id=1, replica_groups=mesh['chip'=8,'core'=2,'expert'=16] {'expert'}, dimensions={0} | all-to-all | bytes 1048576 | tf_op jit(solution)/shard_map/all_to_all | solution.py:9
  49.8 0.9 multiply_convert_fusion.1
  50.8 6.2 %pad_maximum_fusion = bf16[384,8192]{1,0:T(8,128)(2,1)} fusion(bf16[192,8192]{1,0:T(8,128)(2,1)} %bitcast.136, bf16[192,8192]{1,0:T(8,128)(2,1)} %bitcast.137), kind=kLoop, calls=%fused_computation.5 | loop fusion | flops 12582912 | bytes 12582912 | tf_op jit(solution)/shard_map/concatenate | solution.py:98
  57.0 1.0 collective-permute-start.2
  58.0 2.0 collective-permute-done.2
  59.9 30.8 %all-gather.2.cloned.1.call-done = bf16[384,8192]{1,0:T(8,128)(2,1)} async-done(((bf16[24,8192]{1,0:T(8,128)(2,1)}), bf16[384,8192]{1,0:T(8,128)(2,1)}) %all-gather.2.cloned.1.call-update) | async-done | bytes 6291472 | tf_op jit(solution)/shard_map/all_gather | solution.py:97
  90.7 8.2 %fusion.67 = f32[384,384]{0,1:T(8,128)S(1)} fusion(bf16[384,8192]{1,0:T(8,128)(2,1)} %all-gather.2.cloned.1.call-done, bf16[384,8192]{1,0:T(8,128)(2,1)} %pad_maximum_fusion), kind=kOutput, calls=%fused_computation.132 | convolution fusion | flops 2415919104 | bytes 13172736 | tf_op jit(solution)/shard_map/dot_general | solution.py:29
  99.2 0.6 gather_fusion.1
  99.8 2.6 %convolution_convert_fusion = bf16[192,8192]{1,0:T(8,128)(2,1)} fusion(bf16[1,192,8192]{2,1,0:T(8,128)(2,1)S(1)} %copy-done, bf16[2,192,192]{2,1,0:T(8,128)(2,1)S(1)} %bitcast.141, s32[]{:T(128)S(6)} %select_n.116), kind=kOutput, calls=%fused_computation.3 | convolution fusion | flops 605552640 | bytes 6389764 | tf_op jit(solution)/shard_map/dot_general | solution.py:120
  102.6 1.0 convolution_convert_fusion.1
  103.6 4.8 %collective-permute-done.4 = bf16[192,8192]{1,0:T(8,128)(2,1)} collective-permute-done((bf16[192,8192]{1,0:T(8,128)(2,1)}, bf16[192,8192]{1,0:T(8,128)(2,1)}, u32[]{:S(2)}, u32[]{:S(2)}) %collective-permute-start.4) | collective-permute-done | bytes 3145760 | tf_op jit(solution)/shard_map/ppermute | solution.py:128
  108.4 4.6 %add_convert_fusion = bf16[192,8192]{1,0:T(8,128)(2,1)} fusion(bf16[192,8192]{1,0:T(8,128)(2,1)} %collective-permute-done.4, bf16[192,8192]{1,0:T(8,128)(2,1)S(1)} %convolution_convert_fusion.1), kind=kLoop, calls=%fused_computation.6 | loop fusion | flops 6291456 | bytes 9437184 | tf_op jit(solution)/shard_map/convert_element_type | solution.py:130
  113.1 0.5 collective-permute-start.3
  113.5 48.7 %reduce-scatter.2.cloned.1.call-done = bf16[24,8192]{1,0:T(8,128)(2,1)} async-done(((bf16[192,8192]{1,0:T(8,128)(2,1)}), bf16[24,8192]{1,0:T(8,128)(2,1)}) %reduce-scatter.2.cloned.1.call-update) | async-done | bytes 393232 | tf_op jit(solution)/shard_map/reduce_scatter | solution.py:131
  162.3 1.1 multiply_convert_fusion
  163.4 0.8 copy.31
  164.2 9.3 %all-to-all-start.1 = ((bf16[16,24,512]{2,1,0:T(8,128)(2,1)}), bf16[16,24,512]{2,1,0:T(8,128)(2,1)S(1)}, u32[]{:S(2)}, u32[]{:S(2)}) async-start(bf16[16,24,512]{2,1,0:T(8,128)(2,1)} %bitcast.139), calls=%async_computation.2 | async-start | bytes 786432 | tf_op jit(solution)/shard_map/all_to_all | solution.py:134
  173.5 1.6 scatter_custom_fusion
  175.1 11.9 %all-to-all-done.1 = bf16[16,24,512]{2,1,0:T(8,128)(2,1)S(1)} async-done(((bf16[16,24,512]{2,1,0:T(8,128)(2,1)}), bf16[16,24,512]{2,1,0:T(8,128)(2,1)S(1)}, u32[]{:S(2)}, u32[]{:S(2)}) %all-to-all-start.1) | async-done | bytes 393248 | tf_op jit(solution)/shard_map/all_to_all | solution.py:134
  187.0 0.8 fusion.2
  187.8 2.6 %add_convert_fusion.1 = bf16[1024,512]{1,0:T(8,128)(2,1)} fusion(f32[1024,512]{1,0:T(8,128)S(1)} %fusion.2, bf16[1024,512]{1,0:T(8,128)(2,1)} %collective-permute-done.3), kind=kLoop, calls=%fused_computation.9 | loop fusion | flops 1572864 | bytes 4194304 | tf_op jit(solution)/shard_map/convert_element_type | solution.py:143
  (52 shorter events, 2.0 us)
Async XLA Ops:
  6.5 93.2 %copy-start = (bf16[1,192,8192]{2,1,0:T(8,128)(2,1)S(1)}, bf16[1,192,8192]{2,1,0:T(8,128)(2,1)}, u32[]{:S(2)}) copy-start(bf16[1,192,8192]{2,1,0:T(8,128)(2,1)} %param.17) | copy-start | bytes 9437188
  6.5 84.2 %all-gather.2.cloned.1.call-start = ((), (), s32[]{:S(2)}) async-start(), calls=%async_computation.3 | async-start | bytes 6684672 | tf_op jit(solution)/shard_map/all_gather | solution.py:97
  6.5 3.8 %collective-permute-start = (s32[256,1]{0,1:T(1,128)}, s32[256,1]{0,1:T(1,128)S(1)}, u32[]{:S(2)}, u32[]{:S(2)}) collective-permute-start(s32[256,1]{0,1:T(1,128)} %param.12), channel_id=1, source_target_pairs={{16,0},{32,16},{48,32},{64,48},{80,64},{96,80},{112,96},{128,112},... | collective-permute-start | bytes 3080 | tf_op jit(solution)/shard_map/ppermute | solution.py:25
  6.8 7.1 %collective-permute-start.1 = (s32[1,256]{1,0:T(1,128)}, s32[1,256]{1,0:T(1,128)S(1)}, u32[]{:S(2)}, u32[]{:S(2)}) collective-permute-start(s32[1,256]{1,0:T(1,128)} %param.11), channel_id=1, source_target_pairs={{16,0},{32,16},{48,32},{64,48},{80,64},{96,80},{112,96},{128,112},... | collective-permute-start | bytes 3080 | tf_op jit(solution)/shard_map/ppermute | solution.py:25
  50.7 111.6 %reduce-scatter.2.cloned.1.call-start = ((), (), s32[]{:S(2)}) async-start(), calls=%async_computation.4 | async-start | bytes 3538944 | tf_op jit(solution)/shard_map/reduce_scatter | solution.py:131
  57.0 3.0 %collective-permute-start.2 = (f32[24]{0:T(128)S(1)}, f32[24]{0:T(128)S(1)}, u32[]{:S(2)}, u32[]{:S(2)}) collective-permute-start(f32[24]{0:T(128)S(1)} %get-tuple-element.23), channel_id=1, source_target_pairs={{240,0},{0,16},{16,32},{32,48},{48,64},{64,80},{80,96},{96,112},{1... | collective-permute-start | bytes 296 | tf_op jit(solution)/shard_map/ppermute | solution.py:25
  102.4 6.0 %collective-permute-start.4 = (bf16[192,8192]{1,0:T(8,128)(2,1)}, bf16[192,8192]{1,0:T(8,128)(2,1)}, u32[]{:S(2)}, u32[]{:S(2)}) collective-permute-start(bf16[192,8192]{1,0:T(8,128)(2,1)} %convolution_convert_fusion), channel_id=1, source_target_pairs={{0,16},{16,0},{1,17},{17,1},{2,18},{18,2},{3,19},{19,3},{4,20},{20... | collective-permute-start | bytes 9437192 | tf_op jit(solution)/shard_map/ppermute | solution.py:128
  113.0 60.5 %copy-start.1 = (s32[1,256]{1,0:T(1,128)S(1)}, s32[1,256]{1,0:T(1,128)}, u32[]{:S(2)}) copy-start(s32[1,256]{1,0:T(1,128)} %param.11) | copy-start | bytes 3076
  113.1 74.7 %collective-permute-start.3 = (bf16[1024,512]{1,0:T(8,128)(2,1)}, bf16[1024,512]{1,0:T(8,128)(2,1)}, u32[]{:S(2)}, u32[]{:S(2)}) collective-permute-start(bf16[1024,512]{1,0:T(8,128)(2,1)} %param.10), channel_id=1, source_target_pairs={{240,0},{0,16},{16,32},{32,48},{48,64},{64,80},{80,96},{96,112},{1... | collective-permute-start | bytes 3145736 | tf_op jit(solution)/shard_map/ppermute | solution.py:25
  164.2 22.8 %all-to-all-start.1 = ((bf16[16,24,512]{2,1,0:T(8,128)(2,1)}), bf16[16,24,512]{2,1,0:T(8,128)(2,1)S(1)}, u32[]{:S(2)}, u32[]{:S(2)}) async-start(bf16[16,24,512]{2,1,0:T(8,128)(2,1)} %bitcast.139), calls=%async_computation.2 | async-start | bytes 786432 | tf_op jit(solution)/shard_map/all_to_all | solution.py:134
Sparse Core Ops, SparseCore 0:
  50.8 39.8 all-gather.1
  113.2 49.0 reduce-scatter.1
